TPU v7x, 32 devices: a whole 2x2x4 slice. The times are simulated.
32 devices in a mesh: fsdp: 8 (over y, x, core), dp: 4 (over z).
Axes of the slice: x: 2, y: 2, z: 4, core: 2. Of those that a mesh axis runs over, the one named last changes fastest.
Arguments:
- tokens: bfloat16 [131072, 1024], P(('fsdp', 'dp')), may hold values from -6 to 6
- cotangent: bfloat16 [131072, 1024], P(('fsdp', 'dp')), may hold values from -6 to 6
- lengths: int32 [256], P(('fsdp', 'dp')), may hold values from 8 to 2048, as said below
- selected: int32 [16384], P(('fsdp', 'dp')), may hold values from 0 to 4095, as said below
- attn_in: bfloat16 [1024, 3072], P('fsdp'), may hold values from -0.1875 to 0.1875
- attn_out: bfloat16 [1024, 1024], P('fsdp'), may hold values from -0.75 to 0.75
- mlp_in: bfloat16 [1024, 4096], P('fsdp'), may hold values from -0.1875 to 0.1875
- mlp_out: bfloat16 [4096, 1024], P('fsdp'), may hold values from -0.09375 to 0.09375
- norm_attn: bfloat16 [1024], P('fsdp'), may hold values from 0.5 to 1.5
- norm_mlp: bfloat16 [1024], P('fsdp'), may hold values from 0.5 to 1.5
- router: bfloat16 [1024], replicated, may hold values from -0.1875 to 0.1875
Outputs:
- output: bfloat16 [131072, 1024], P(('fsdp', 'dp'))
- grad_tokens: bfloat16 [131072, 1024], P(('fsdp', 'dp'))
- grad_attn_in: float32 [1024, 3072], P('fsdp')
- grad_attn_out: float32 [1024, 1024], P('fsdp')
- grad_mlp_in: float32 [1024, 4096], P('fsdp')
- grad_mlp_out: float32 [4096, 1024], P('fsdp')
- grad_norm_attn: float32 [1024], P('fsdp')
- grad_norm_mlp: float32 [1024], P('fsdp')
- grad_router: float32 [1024], replicated
Inputs may be any that keep to these rules, and one draw needn't show every extreme that they name: `lengths`: each aligned block of 8 entries (one device's sequences, in order) holds multiples of 8 that sum to 4096; exactly one of them equals 2048. `selected`: each aligned block of 512 entries lists distinct positions within its device's 4096 tokens in ascending order; a sequence of length L has exactly L / 8 of its positions listed.
All inputs are finite; a program needn't handle non-finite values.
Results may differ from a plain program's by a relative error of at most 0.014.
Values may be sent and summed in bfloat16 or wider, within the bound.
No kernel may reach another device: no remote copies, remote signals or barrier semaphores. Data moves between devices by JAX's collectives and lax.ppermute only.
A program may use at most 192 MiB of HBM per device.

v0:
```python
import jax
import jax.numpy as jnp
from jax import lax
from jax.sharding import PartitionSpec as P

HEADS = 16
HEAD = 64
EPS = 1e-06
MASKED = -1e30


def rms_scale(values, gain_vec):
    return values * lax.rsqrt(jnp.mean(values * values, axis=-1, keepdims=True) + EPS) * gain_vec


def seq_mask(lengths, selected):
    seq_ends = jnp.cumsum(lengths)
    owner_seq = jnp.sum((selected[:, None] >= seq_ends[None, :]).astype(jnp.int32), axis=1)
    return (owner_seq[:, None] == owner_seq[None, :]) & (selected[None, :] <= selected[:, None])


def split_heads(matrix):
    return matrix.reshape(matrix.shape[0], HEADS, HEAD)


def masked_scores(query_heads, key_heads, allowed, score_scale):
    scores = (
        jnp.einsum("qhd,khd->hqk", query_heads, key_heads, preferred_element_type=jnp.float32)
        * score_scale
    )
    return jnp.where(allowed[None], scores, MASKED)


def per_device(
    tokens,
    cotangent,
    lengths,
    selected,
    attn_in,
    attn_out,
    mlp_in,
    mlp_out,
    norm_attn,
    norm_mlp,
    router,
):
    model_width = tokens.shape[1]
    row_count = selected.shape[0]
    score_scale = HEAD ** (-0.5)
    w_qkv, w_out, gain_attn, gain_mlp = (
        lax.all_gather(attn_in, "fsdp", axis=0, tiled=True),
        lax.all_gather(attn_out, "fsdp", axis=0, tiled=True),
        lax.all_gather(norm_attn, "fsdp", axis=0, tiled=True),
        lax.all_gather(norm_mlp, "fsdp", axis=0, tiled=True),
    )
    w_in, w_down = (
        lax.all_gather(mlp_in, "fsdp", axis=0, tiled=True),
        lax.all_gather(mlp_out, "fsdp", axis=0, tiled=True),
    )
    gain_one = gain_attn.astype(jnp.float32)
    gain_two = gain_mlp.astype(jnp.float32)
    positions = lax.broadcasted_iota(jnp.int32, (row_count, tokens.shape[0]), 1)
    select = (selected[:, None] == positions).astype(jnp.bfloat16)
    routed = jnp.dot(select, tokens, preferred_element_type=jnp.float32)
    routed_low = routed.astype(jnp.bfloat16)
    router_rate = jnp.dot(routed_low, router, preferred_element_type=jnp.float32)
    allowed = seq_mask(lengths, selected)
    normed_float, norm_pull = jax.vjp(rms_scale, routed, gain_one)
    normed = normed_float.astype(jnp.bfloat16)
    qkv = jnp.dot(normed, w_qkv, preferred_element_type=jnp.float32).astype(jnp.bfloat16)
    query_heads = split_heads(qkv[:, :model_width])
    key_heads = split_heads(qkv[:, model_width : 2 * model_width])
    value_heads = split_heads(qkv[:, 2 * model_width :])
    scores = masked_scores(query_heads, key_heads, allowed, score_scale)
    highest = jnp.max(scores, axis=-1, keepdims=True)
    exponent = jnp.exp(scores - highest)
    row_total = jnp.sum(exponent, axis=-1, keepdims=True)
    probabilities = (exponent / row_total).astype(jnp.bfloat16)
    log_total = highest + jnp.log(row_total)
    attn_mix = jnp.einsum(
        "hqk,khd->qhd", probabilities, value_heads, preferred_element_type=jnp.float32
    )
    attn_mix = attn_mix.reshape(row_count, model_width).astype(jnp.bfloat16)
    attended = jnp.dot(attn_mix, w_out, preferred_element_type=jnp.float32)
    middle = routed + attended
    normed_two_float, middle_pull = jax.vjp(rms_scale, middle, gain_two)
    normed_two = normed_two_float.astype(jnp.bfloat16)
    pre_gelu = jnp.dot(normed_two, w_in, preferred_element_type=jnp.float32)
    active_float, gelu_pull = jax.vjp(jax.nn.gelu, pre_gelu)
    active = active_float.astype(jnp.bfloat16)
    expanded = jnp.dot(active, w_down, preferred_element_type=jnp.float32)
    update = attended + expanded
    branch = (router_rate[:, None] * update).astype(jnp.bfloat16)
    output = (
        tokens.astype(jnp.float32)
        + jnp.einsum("kt,kd->td", select, branch, preferred_element_type=jnp.float32)
    ).astype(jnp.bfloat16)
    w_qkv_back, w_out_back = (
        lax.all_gather(attn_in, "fsdp", axis=0, tiled=True),
        lax.all_gather(attn_out, "fsdp", axis=0, tiled=True),
    )
    w_in_back, w_down_back = (
        lax.all_gather(mlp_in, "fsdp", axis=0, tiled=True),
        lax.all_gather(mlp_out, "fsdp", axis=0, tiled=True),
    )
    cot_rows = jnp.dot(select, cotangent, preferred_element_type=jnp.float32)
    grad_rate = jnp.sum(cot_rows * update, axis=-1)
    grad_update = cot_rows * router_rate[:, None]
    grad_expanded = grad_update.astype(jnp.bfloat16)
    grad_down = jnp.einsum("kf,kd->fd", active, grad_expanded, preferred_element_type=jnp.float32)
    grad_active = jnp.einsum(
        "kd,fd->kf", grad_expanded, w_down_back, preferred_element_type=jnp.float32
    )
    (grad_inner_float,) = gelu_pull(grad_active)
    grad_inner = grad_inner_float.astype(jnp.bfloat16)
    grad_up = jnp.einsum("kd,kf->df", normed_two, grad_inner, preferred_element_type=jnp.float32)
    grad_normed_two = jnp.einsum(
        "kf,df->kd", grad_inner, w_in_back, preferred_element_type=jnp.float32
    )
    grad_middle, grad_gain_two = middle_pull(grad_normed_two)
    grad_attended = (grad_update + grad_middle).astype(jnp.bfloat16)
    grad_proj = jnp.einsum("ka,kd->ad", attn_mix, grad_attended, preferred_element_type=jnp.float32)
    grad_mix = jnp.einsum(
        "kd,ad->ka", grad_attended, w_out_back, preferred_element_type=jnp.float32
    ).astype(jnp.bfloat16)
    grad_mix_heads = split_heads(grad_mix)
    scores_again = masked_scores(query_heads, key_heads, allowed, score_scale)
    prob_float = jnp.where(allowed[None], jnp.exp(scores_again - log_total), 0.0)
    grad_probs = jnp.einsum(
        "qhd,khd->hqk", grad_mix_heads, value_heads, preferred_element_type=jnp.float32
    )
    row_delta = jnp.sum(prob_float * grad_probs, axis=-1, keepdims=True)
    grad_scores = (prob_float * (grad_probs - row_delta)).astype(jnp.bfloat16)
    prob_low = prob_float.astype(jnp.bfloat16)
    grad_query = (
        jnp.einsum("hqk,khd->qhd", grad_scores, key_heads, preferred_element_type=jnp.float32)
        * score_scale
    )
    grad_key = (
        jnp.einsum("hqk,qhd->khd", grad_scores, query_heads, preferred_element_type=jnp.float32)
        * score_scale
    )
    grad_value = jnp.einsum(
        "hqk,qhd->khd", prob_low, grad_mix_heads, preferred_element_type=jnp.float32
    )
    grad_qkv = jnp.concatenate(
        [
            grad_query.reshape(row_count, model_width),
            grad_key.reshape(row_count, model_width),
            grad_value.reshape(row_count, model_width),
        ],
        axis=1,
    ).astype(jnp.bfloat16)
    grad_proj_in = jnp.einsum("kd,ke->de", normed, grad_qkv, preferred_element_type=jnp.float32)
    grad_normed = jnp.einsum("ke,de->kd", grad_qkv, w_qkv_back, preferred_element_type=jnp.float32)
    grad_routed_norm, grad_gain_one = norm_pull(grad_normed)
    grad_routed = (
        grad_routed_norm + grad_middle + grad_rate[:, None] * router.astype(jnp.float32)
    ).astype(jnp.bfloat16)
    grad_tokens = (
        cotangent.astype(jnp.float32)
        + jnp.einsum("kt,kd->td", select, grad_routed, preferred_element_type=jnp.float32)
    ).astype(jnp.bfloat16)
    router_local = jnp.dot(grad_rate, routed, precision=lax.Precision.HIGHEST)
    shard_up, shard_down, shard_gain_two = (
        lax.psum_scatter(grad_up, "fsdp", scatter_dimension=0, tiled=True),
        lax.psum_scatter(grad_down, "fsdp", scatter_dimension=0, tiled=True),
        lax.psum_scatter(grad_gain_two, "fsdp", scatter_dimension=0, tiled=True),
    )
    shard_qkv, shard_proj, shard_gain_one = (
        lax.psum_scatter(grad_proj_in, "fsdp", scatter_dimension=0, tiled=True),
        lax.psum_scatter(grad_proj, "fsdp", scatter_dimension=0, tiled=True),
        lax.psum_scatter(grad_gain_one, "fsdp", scatter_dimension=0, tiled=True),
    )
    summed = (
        lax.psum(shard_qkv.astype(jnp.bfloat16), "dp").astype(jnp.float32),
        lax.psum(shard_proj.astype(jnp.bfloat16), "dp").astype(jnp.float32),
        lax.psum(shard_up.astype(jnp.bfloat16), "dp").astype(jnp.float32),
        lax.psum(shard_down.astype(jnp.bfloat16), "dp").astype(jnp.float32),
        lax.psum(shard_gain_one.astype(jnp.bfloat16), "dp").astype(jnp.float32),
        lax.psum(shard_gain_two.astype(jnp.bfloat16), "dp").astype(jnp.float32),
    )
    grad_router = lax.psum(router_local, ("fsdp", "dp"))
    return (
        output,
        grad_tokens,
        summed[0],
        summed[1],
        summed[2],
        summed[3],
        summed[4],
        summed[5],
        grad_router,
    )


def solution(mesh):
    placed = (
        P(("fsdp", "dp"), None),
        P(("fsdp", "dp"), None),
        P(("fsdp", "dp")),
        P(("fsdp", "dp")),
        P("fsdp", None),
        P("fsdp", None),
        P("fsdp", None),
        P("fsdp", None),
        P("fsdp"),
        P("fsdp"),
        P(),
    )
    return jax.shard_map(
        per_device,
        mesh=mesh,
        in_specs=placed,
        out_specs=(
            P(("fsdp", "dp"), None),
            P(("fsdp", "dp"), None),
            P("fsdp", None),
            P("fsdp", None),
            P("fsdp", None),
            P("fsdp", None),
            P("fsdp"),
            P("fsdp"),
            P(),
        ),
        check_vma=False,
    )
```

profile of v0, /device:TPU:0, one launch (start us, length us, event | category | flops | bytes accessed | tf_op | source)
XLA Modules:
  0.0 773.5 jit_solution(13917479941379814595)
XLA Ops:
  10.0 10.4 %all-gather = bf16[8,1,128]{2,1,0:T(2,128)(2,1)S(1)} all-gather(bf16[1,1,128]{2,1,0:T(2,128)(2,1)} %bitcast.84), channel_id=1, replica_groups=mesh['fsdp'=8,'dp'=4] {'fsdp'}, dimensions={0}, use_global_device_ids=true | all-gather | bytes 2304 | tf_op jit(solution)/shard_map/all_gather | solution.py:53
  20.4 8.9 %all-gather.1 = bf16[8,1,128]{2,1,0:T(2,128)(2,1)S(1)} all-gather(bf16[1,1,128]{2,1,0:T(2,128)(2,1)} %bitcast.85), channel_id=1, replica_groups=mesh['fsdp'=8,'dp'=4] {'fsdp'}, dimensions={0}, use_global_device_ids=true | all-gather | bytes 2304 | tf_op jit(solution)/shard_map/all_gather | solution.py:54
  31.6 7.8 %multiply_reduce_fusion.7 = (f32[512]{0:T(512)S(1)}, f32[512,1024]{1,0:T(8,128)S(1)}) fusion(bf16[4096,1024]{1,0:T(8,128)(2,1)} %param.11, s32[512]{0:T(512)} %param.14), kind=kOutput, calls=%fused_computation.51 | convolution fusion | flops 4298112512 | bytes 10489856 | tf_op jit(solution)/shard_map/dot_general | solution.py:64
  40.1 9.3 %fusion.12 = f32[512,1024]{1,0:T(8,128)} fusion(bf16[4096,1024]{1,0:T(8,128)(2,1)} %param.12, s32[512]{0:T(512)S(1)} %copy-done.10), kind=kOutput, calls=%fused_computation.24 | convolution fusion | flops 4297064448 | bytes 10487808 | tf_op jit(solution)/shard_map/dot_general | solution.py:106
  49.4 8.7 %all-gather.7.cloned.1.call-done = bf16[1024,3072]{1,0:T(8,128)(2,1)} async-done(((bf16[128,3072]{1,0:T(8,128)(2,1)}), bf16[1024,3072]{1,0:T(8,128)(2,1)}) %all-gather.7.cloned.1.call-update) | async-done | bytes 6291472 | tf_op jit(solution)/shard_map/all_gather | solution.py:51
  58.0 6.6 convolution_convert_fusion
  72.4 9.1 %fusion.1 = (f32[16,512]{1,0:T(8,128)S(1)}, f32[16,512,512]{1,2,0:T(8,128)}) fusion(pred[512,512]{0,1:T(8,128)(4,1)S(1)} %compare_and_fusion, bf16[512,16,64]{0,2,1:T(8,128)(2,1)} %bitcast.57, bf16[512,16,64]{0,2,1:T(8,128)(2,1)S(1)} %bitcast.55), kind=kOutput, calls=%fused_computation.11 | convolution fusion | flops 549445632 | bytes 19169280 | tf_op jit(solution)/shard_map/qhd,khd->hqk/dot_general | solution.py:28
  81.5 9.3 %fusion = f32[16,512]{1,0:T(8,128)S(1)} fusion(f32[16,512,512]{1,2,0:T(8,128)} %get-tuple-element.31, f32[16,512]{1,0:T(8,128)S(1)} %get-tuple-element.30, pred[512,512]{0,1:T(8,128)(4,1)S(1)} %compare_and_fusion), kind=kLoop, calls=%fused_computation.8 | loop fusion | flops 16769024 | bytes 17104896 | tf_op jit(solution)/shard_map/reduce_sum | solution.py:77
  90.8 9.6 %fusion.23 = bf16[16,64,512]{2,1,0:T(8,128)(2,1)} fusion(bf16[512,16,64]{0,2,1:T(8,128)(2,1)} %bitcast.65, f32[16,512,512]{1,2,0:T(8,128)} %get-tuple-element.31, f32[16,512]{1,0:T(8,128)S(1)} %fusion, f32[16,512]{1,0:T(8,128)S(1)} %get-tuple-element.30, pred[512,512]{0,1:T(8,128)(4,1)S(1)} %compare_and_fusion), kind=kOutput, calls=%fused_computation.54 | convolution fusion | flops 558366720 | bytes 19202048 | tf_op jit(solution)/shard_map/hqk,khd->qhd/dot_general | solution.py:80
  100.4 5.2 multiply_reduce_fusion.6
  105.6 38.3 %all-gather.11.cloned.1.call-done = bf16[1024,4096]{1,0:T(8,128)(2,1)} async-done(((bf16[128,4096]{1,0:T(8,128)(2,1)}), bf16[1024,4096]{1,0:T(8,128)(2,1)}) %all-gather.11.cloned.1.call-update) | async-done | bytes 8388624 | tf_op jit(solution)/shard_map/all_gather | solution.py:57
  143.9 12.1 %fusion.50 = f32[512,4096]{1,0:T(8,128)} fusion(bf16[1024,4096]{1,0:T(8,128)(2,1)} %all-gather.11.cloned.1.call-done, f32[512,1024]{1,0:T(8,128)} %get-tuple-element.22, f32[1024]{0:T(1024)S(1)} %bitcast.74, f32[512]{0:T(512)S(1)} %fusion.39), kind=kOutput, calls=%fused_computation.88 | convolution fusion | flops 4296540160 | bytes 18880512 | tf_op jit(solution)/shard_map/dot_general | solution.py:88
  156.0 44.0 %all-gather.13.cloned.1.call-done = bf16[4096,1024]{1,0:T(8,128)(2,1)} async-done(((bf16[512,1024]{1,0:T(8,128)(2,1)}), bf16[4096,1024]{1,0:T(8,128)(2,1)}) %all-gather.13.cloned.1.call-update) | async-done | bytes 8388624 | tf_op jit(solution)/shard_map/all_gather | solution.py:58
  200.0 14.6 %fusion.8 = bf16[512,4096]{1,0:T(8,128)(2,1)} fusion(f32[512,4096]{1,0:T(8,128)} %fusion.50, bf16[4096,1024]{1,0:T(8,128)(2,1)} %all-gather.13.cloned.1.call-done, f32[512,1024]{1,0:T(8,128)} %fusion.12, f32[512]{0:T(512)S(1)} %bitcast.79), kind=kOutput, calls=%fused_computation.18 | convolution fusion | flops 4337958912 | bytes 23070720 | tf_op jit(solution)/shard_map/kd,fd->kf/dot_general | solution.py:111
  214.6 10.9 %multiply_reduce_fusion.1 = (f32[1024]{0:T(1024)S(1)}, f32[512]{0:T(512)S(1)}, f32[512,1024]{1,0:T(8,128)}) fusion(f32[512,1024]{1,0:T(8,128)S(1)} %copy-done.1, f32[512]{0:T(512)S(1)} %fusion.39, f32[1024]{0:T(1024)S(1)} %bitcast.75, bf16[512,4096]{1,0:T(8,128)(2,1)} %fusion.8, bf16[1024,4096]{1,0:T(8,128)(2,1)} %all-gather.11.cloned.1.call-done), kind=kOutput, calls=%fused_computation.39 | convolution fusion | flops 4298111488 | bytes 16789504 | tf_op jit(solution)/shard_map/kf,df->kd/dot_general | solution.py:117
  225.5 10.1 %multiply_reduce_fusion.3 = (f32[512]{0:T(512)S(1)}, bf16[512,1024]{1,0:T(8,128)(2,1)S(1)}, f32[512,1024]{1,0:T(8,128)}) fusion(f32[512,1024]{1,0:T(8,128)S(1)} %copy-done.19, f32[512,1024]{1,0:T(8,128)S(1)} %copy-done.1, f32[512]{0:T(512)S(1)} %multiply_multiply_fusion.3, f32[512]{0:T(512)S(1)} %fusion.39, f32[512,1024]{1,0:T(8,128)} %get-tuple-element.33, ...), kind=kOutput, calls=%fused_computation.41 | convolution fusion | flops 4319608320 | bytes 28323840 | tf_op jit(solution)/shard_map/dot_general | solution.py:91
  239.8 4.2 convolution_convert_fusion.1
  246.4 13.6 %multiply_reduce_fusion = (f32[16,512]{1,0:T(8,128)S(1)}, f32[16,512,512]{1,2,0:T(8,128)}) fusion(f32[16,512]{1,0:T(8,128)S(1)} %log_add_fusion, f32[16,512,512]{1,2,0:T(8,128)} %get-tuple-element.31, pred[512,512]{0,1:T(8,128)(4,1)S(1)} %compare_and_fusion, bf16[512,16,64]{0,2,1:T(8,128)(2,1)} %bitcast.67, bf16[512,16,64]{0,2,1:T(8,128)(2,1)} %bitcast.66), kind=kOutput, calls=%fused_computation.2 | convolution fusion | flops 562028544 | bytes 35979264 | tf_op jit(solution)/shard_map/qhd,khd->hqk/dot_general | solution.py:129
  259.9 13.2 %multiply_convert_fusion = bf16[16,512,512]{1,2,0:T(8,128)(2,1)S(1)} fusion(f32[16,512,512]{1,2,0:T(8,128)} %get-tuple-element.36, f32[16,512]{1,0:T(8,128)S(1)} %get-tuple-element.35, f32[16,512]{1,0:T(8,128)S(1)} %log_add_fusion, f32[16,512,512]{1,2,0:T(8,128)} %get-tuple-element.31, pred[512,512]{0,1:T(8,128)(4,1)S(1)} %compare_and_fusion), kind=kLoop, calls=%fused_computation.1 | loop fusion | flops 29360128 | bytes 42270720 | tf_op jit(solution)/shard_map/convert_element_type | solution.py:133
  277.4 8.6 %fusion.24 = bf16[16,64,512]{2,1,0:T(8,128)(2,1)S(1)} fusion(bf16[512,16,64]{0,2,1:T(8,128)(2,1)S(1)} %bitcast.68, f32[16,512]{1,0:T(8,128)S(1)} %log_add_fusion, f32[16,512,512]{1,2,0:T(8,128)} %get-tuple-element.31, pred[512,512]{0,1:T(8,128)(4,1)S(1)} %compare_and_fusion), kind=kOutput, calls=%fused_computation.56 | convolution fusion | flops 558366720 | bytes 19169280 | tf_op jit(solution)/shard_map/hqk,qhd->khd/dot_general | solution.py:143
  287.0 9.9 %fusion.27 = f32[1024,3072]{1,0:T(8,128)} fusion(bf16[512,1024]{0,1:T(8,128)(2,1)S(1)} %bitcast.88, bf16[512,1024]{0,1:T(8,128)(2,1)S(1)} %bitcast.63, bf16[512,1024]{0,1:T(8,128)(2,1)S(1)} %bitcast.59, f32[512,1024]{1,0:T(8,128)S(1)} %get-tuple-element.29, f32[1024]{0:T(1024)S(1)} %bitcast.71, f32[512]{0:T(512)S(1)} %fusion.38), kind=kOutput, calls=%fused_computation.57 | convolution fusion | flops 3232235520 | bytes 17831936 | tf_op jit(solution)/shard_map/kd,ke->de/dot_general | solution.py:154
  296.9 19.0 %fusion.47 = f32[4096,1024]{1,0:T(8,128)} fusion(f32[512,1024]{1,0:T(8,128)} %fusion.12, f32[512]{0:T(512)S(1)} %bitcast.81, f32[512,4096]{1,0:T(8,128)} %fusion.50), kind=kOutput, calls=%fused_computation.85 | convolution fusion | flops 4314890240 | bytes 27265024 | tf_op jit(solution)/shard_map/kf,kd->fd/dot_general | solution.py:110
  316.2 15.3 %fusion.49 = f32[1024,4096]{1,0:T(8,128)} fusion(bf16[512,4096]{1,0:T(8,128)(2,1)} %fusion.8, f32[512,1024]{1,0:T(8,128)} %get-tuple-element.22, f32[1024]{0:T(1024)S(1)} %bitcast.77, f32[512]{0:T(512)S(1)} %fusion.39), kind=kOutput, calls=%fused_computation.87 | convolution fusion | flops 4296540160 | bytes 23074816 | tf_op jit(solution)/shard_map/kd,kf->df/dot_general | solution.py:116
  333.5 8.4 %multiply_reduce_fusion.2 = (f32[1024]{0:T(1024)S(1)}, f32[512]{0:T(512)S(1)}, f32[512,1024]{1,0:T(8,128)}) fusion(f32[512,1024]{1,0:T(8,128)S(1)} %get-tuple-element.29, f32[512]{0:T(512)S(1)} %fusion.38, f32[1024]{0:T(1024)S(1)} %bitcast.72, bf16[1024,3072]{1,0:T(8,128)(2,1)} %all-gather.7.cloned.1.call-done, bf16[512,1024]{0,1:T(8,128)(2,1)} %bitcast.89, ...), kind=kOutput, calls=%fused_computation.40 | convolution fusion | flops 3233806848 | bytes 13643776 | tf_op jit(solution)/shard_map/ke,de->kd/dot_general | solution.py:155
  341.9 15.5 %all-reduce.2 = (bf16[1024]{0:T(1024)(128)(2,1)S(1)}, bf16[1024]{0:T(1024)(128)(2,1)S(1)}) all-reduce(f32[1024]{0:T(1024)S(1)} %get-tuple-element.11, f32[1024]{0:T(1024)S(1)} %get-tuple-element.9), channel_id=6, replica_groups=mesh['fsdp'=8,'dp'=4] {'fsdp'}, use_global_device_ids=true, to_apply=%region_19.20.clone | all-reduce | flops 2048 | bytes 12288
  357.6 11.7 %all-reduce.3 = (bf16[128]{0:T(256)(128)(2,1)S(1)}, bf16[128]{0:T(256)(128)(2,1)S(1)}) all-reduce(bf16[128]{0:T(256)(128)(2,1)S(1)} %dynamic-slice.7, bf16[128]{0:T(256)(128)(2,1)S(1)} %dynamic-slice.6), channel_id=1, replica_groups=mesh['fsdp'=8,'dp'=4] {'dp'}, use_global_device_ids=true, to_apply=%region_20.21 | all-reduce | flops 256 | bytes 1024 | tf_op jit(solution)/shard_map/psum | solution.py:180
  371.4 37.7 %psum.55 = f32[1024]{0:T(1024)} all-reduce(f32[1024]{0:T(1024)S(1)} %bitcast.69), channel_id=1, replica_groups=mesh['fsdp'=8,'dp'=4] {'fsdp','dp'}, use_global_device_ids=true, to_apply=%region_24.25 | all-reduce | flops 1024 | bytes 8192 | tf_op jit(solution)/shard_map/psum | solution.py:183
  413.7 100.4 %reduce-scatter.11.cloned.1.call-done = f32[512,1024]{1,0:T(8,128)} async-done(((f32[4096,1024]{1,0:T(8,128)}), f32[512,1024]{1,0:T(8,128)}) %reduce-scatter.11.cloned.1.call-update) | async-done | bytes 2097168 | tf_op jit(solution)/shard_map/reduce_scatter | solution.py:167
  516.8 117.0 %reduce-scatter.9.cloned.1.call-done = f32[128,4096]{1,0:T(8,128)} async-done(((f32[1024,4096]{1,0:T(8,128)}), f32[128,4096]{1,0:T(8,128)}) %reduce-scatter.9.cloned.1.call-update) | async-done | bytes 2097168 | tf_op jit(solution)/shard_map/reduce_scatter | solution.py:166
  636.6 10.0 %add_convert_fusion.1 = bf16[4096,1024]{1,0:T(8,128)(2,1)} fusion(bf16[4096,1024]{1,0:T(8,128)(2,1)} %param.11, s32[512]{0:T(512)S(1)} %copy-done.11, f32[512,1024]{1,0:T(8,128)} %get-tuple-element.34, f32[512]{0:T(512)S(1)} %bitcast.82), kind=kOutput, calls=%fused_computation.4 | convolution fusion | flops 4310695936 | bytes 18878464 | tf_op jit(solution)/shard_map/kt,kd->td/dot_general | solution.py:96
  646.6 11.4 %add_convert_fusion = bf16[4096,1024]{1,0:T(8,128)(2,1)} fusion(bf16[4096,1024]{1,0:T(8,128)(2,1)} %param.12, s32[512]{0:T(512)S(1)} %copy-done.11, f32[512,1024]{1,0:T(8,128)S(1)} %get-tuple-element.29, f32[512,1024]{1,0:T(8,128)S(1)} %copy-done.20, f32[1024]{0:T(1024)S(1)} %convert_element_type.135, f32[512]{0:T(512)S(1)} %get-tuple-element.26, ...), kind=kOutput, calls=%fused_computation | convolution fusion | flops 4316987392 | bytes 25190400 | tf_op jit(solution)/shard_map/kt,kd->td/dot_general | solution.py:162
  658.0 100.1 %all-reduce.7.cloned.1.call-done = (bf16[128,3072]{1,0:T(8,128)(2,1)}, bf16[128,1024]{1,0:T(8,128)(2,1)}, bf16[128,4096]{1,0:T(8,128)(2,1)}, bf16[512,1024]{1,0:T(8,128)(2,1)}) async-done(((bf16[128,3072]{1,0:T(8,128)(2,1)}, bf16[128,1024]{1,0:T(8,128)(2,1)}, bf16[128,4096]{1,0:T(8,128)(2,1)}, bf16[512,1024]{1,0:T(8,128)(2,1)}), (bf16[128,3072]{1,0:T(8,128)(2,1)}, bf16[128,1024]{1,0:T(8,128)(2,1)}, ...) | async-done | bytes 3145744 | tf_op jit(solution)/shard_map/psum | solution.py:176
  (100 shorter events, 47.8 us)
Async XLA Ops:
  7.2 50.9 %all-gather.7.cloned.1.call-start = ((), (), s32[]{:S(2)}) async-start(), calls=%async_computation.4 | async-start | bytes 7077888 | tf_op jit(solution)/shard_map/all_gather | solution.py:51
  7.9 92.5 %all-gather.9.cloned.1.call-start = ((), (), s32[]{:S(2)}) async-start(), calls=%async_computation.5 | async-start | bytes 2359296 | tf_op jit(solution)/shard_map/all_gather | solution.py:52
  8.7 135.3 %all-gather.11.cloned.1.call-start = ((), (), s32[]{:S(2)}) async-start(), calls=%async_computation.6 | async-start | bytes 9437184 | tf_op jit(solution)/shard_map/all_gather | solution.py:57
  9.4 190.6 %all-gather.13.cloned.1.call-start = ((), (), s32[]{:S(2)}) async-start(), calls=%async_computation.7 | async-start | bytes 9437184 | tf_op jit(solution)/shard_map/all_gather | solution.py:58
  10.0 399.2 %reduce-scatter.7.cloned.1.call-start = ((), (), s32[]{:S(2)}) async-start(), calls=%async_computation.9 | async-start | bytes 4718592 | tf_op jit(solution)/shard_map/reduce_scatter | solution.py:172
  31.6 7.8 %copy-start.10 = (s32[512]{0:T(512)S(1)}, s32[512]{0:T(512)}, u32[]{:S(2)}) copy-start(s32[512]{0:T(512)} %param.14) | copy-start | bytes 6148
  39.4 0.7 copy-start.13
  200.0 14.6 %copy-start.1 = (f32[512,1024]{1,0:T(8,128)S(1)}, f32[512,1024]{1,0:T(8,128)}, u32[]{:S(2)}) copy-start(f32[512,1024]{1,0:T(8,128)} %get-tuple-element.22) | copy-start | bytes 6291460
  214.6 10.9 %copy-start.3 = (f32[512,1024]{1,0:T(8,128)S(1)}, f32[512,1024]{1,0:T(8,128)}, u32[]{:S(2)}) copy-start(f32[512,1024]{1,0:T(8,128)} %get-tuple-element.32) | copy-start | bytes 6291460
  214.6 10.9 %copy-start.15 = (bf16[4096,1024]{1,0:T(8,128)(2,1)S(1)}, bf16[4096,1024]{1,0:T(8,128)(2,1)}, u32[]{:S(2)}) copy-start(bf16[4096,1024]{1,0:T(8,128)(2,1)} %all-gather.13.cloned.1.call-done) | copy-start | bytes 25165828
  214.6 10.9 %copy-start.19 = (f32[512,1024]{1,0:T(8,128)S(1)}, f32[512,1024]{1,0:T(8,128)}, u32[]{:S(2)}) copy-start(f32[512,1024]{1,0:T(8,128)} %fusion.12) | copy-start | bytes 6291460
  225.5 11.1 %copy-start.6 = (bf16[16,64,512]{2,1,0:T(8,128)(2,1)S(1)}, bf16[16,64,512]{2,1,0:T(8,128)(2,1)}, u32[]{:S(2)}) copy-start(bf16[16,64,512]{2,1,0:T(8,128)(2,1)} %fusion.23) | copy-start | bytes 3145732
  235.6 1.0 copy-start.18
  246.3 164.7 %reduce-scatter.5.cloned.1.call-start = ((), (), s32[]{:S(2)}) async-start(), calls=%async_computation.8 | async-start | bytes 14155776 | tf_op jit(solution)/shard_map/reduce_scatter | solution.py:171
  259.9 13.2 %copy-start = (bf16[512,1024]{0,1:T(8,128)(2,1)S(1)}, bf16[512,1024]{0,1:T(8,128)(2,1)}, u32[]{:S(2)}) copy-start(bf16[512,1024]{0,1:T(8,128)(2,1)} %copy.49) | copy-start | bytes 3145732
  275.7 10.3 %copy-start.7 = (bf16[16,64,512]{2,1,0:T(8,128)(2,1)}, bf16[16,64,512]{2,1,0:T(8,128)(2,1)S(1)}, u32[]{:S(2)}) copy-start(bf16[16,64,512]{2,1,0:T(8,128)(2,1)S(1)} %multiply_convert_fusion.2) | copy-start | bytes 3145732
  275.8 1.6 copy-start.9
  277.4 8.7 %copy-start.4 = (bf16[16,64,512]{2,1,0:T(8,128)(2,1)}, bf16[16,64,512]{2,1,0:T(8,128)(2,1)S(1)}, u32[]{:S(2)}) copy-start(bf16[16,64,512]{2,1,0:T(8,128)(2,1)S(1)} %multiply_convert_fusion.3) | copy-start | bytes 3145732
  286.0 1.0 copy-start.16
  296.9 217.2 %reduce-scatter.11.cloned.1.call-start = ((), (), s32[]{:S(2)}) async-start(), calls=%async_computation.11 | async-start | bytes 18874368 | tf_op jit(solution)/shard_map/reduce_scatter | solution.py:167
  316.0 317.8 %reduce-scatter.9.cloned.1.call-start = ((), (), s32[]{:S(2)}) async-start(), calls=%async_computation.10 | async-start | bytes 18874368 | tf_op jit(solution)/shard_map/reduce_scatter | solution.py:166
  331.5 0.7 copy-start.12
  331.5 0.7 copy-start.17
  331.5 1.9 copy-start.5
  331.6 426.6 %all-reduce.7.cloned.1.call-start = ((), (), s32[]{:S(2)}) async-start(), calls=%async_computation.12 | async-start | bytes 6291456 | tf_op jit(solution)/shard_map/psum | solution.py:176
  333.5 75.7 %copy-start.14 = (f32[512]{0:T(512)S(1)}, f32[512]{0:T(512)}, u32[]{:S(2)}) copy-start(f32[512]{0:T(512)} %copy-done.13) | copy-start | bytes 6148
  409.2 227.4 %copy-start.11 = (s32[512]{0:T(512)S(1)}, s32[512]{0:T(512)}, u32[]{:S(2)}) copy-start(s32[512]{0:T(512)} %param.14) | copy-start | bytes 6148
  636.5 10.1 %copy-start.2 = (f32[512,1024]{1,0:T(8,128)S(1)}, f32[512,1024]{1,0:T(8,128)}, u32[]{:S(2)}) copy-start(f32[512,1024]{1,0:T(8,128)} %get-tuple-element.22) | copy-start | bytes 6291460
  636.6 10.1 %copy-start.20 = (f32[512,1024]{1,0:T(8,128)S(1)}, f32[512,1024]{1,0:T(8,128)}, u32[]{:S(2)}) copy-start(f32[512,1024]{1,0:T(8,128)} %get-tuple-element.37) | copy-start | bytes 6291460
  636.6 10.0 %copy-start.21 = (f32[512,1024]{1,0:T(8,128)S(1)}, f32[512,1024]{1,0:T(8,128)}, u32[]{:S(2)}) copy-start(f32[512,1024]{1,0:T(8,128)} %get-tuple-element.33) | copy-start | bytes 6291460
  758.1 7.1 copy-start.8
Sparse Core Ops, SparseCore 0:
  9.9 48.1 all-gather.6
  59.9 27.7 all-gather.8
  89.6 54.2 all-gather.10
  145.7 54.2 all-gather.12
  246.4 51.1 reduce-scatter.6
  301.0 93.5 reduce-scatter.4
  398.2 115.8 reduce-scatter.10
  517.6 116.1 reduce-scatter.8
  637.0 121.0 all-reduce.6
where the time goes:
time: 783 us; the launch traced here: 774 us
  waiting for transfers between devices  411 us (52%)
  matrix products  204 us (26%)
  blocking collectives  84.2 us (11%)
  other arithmetic  44 us (6%)
  between operations  15 us (2%)
  local copies, waits for them, and re-layouts  14.3 us (2%)
    reduce_scatter x1, waiting for transfers between devices, per_device(): lax.psum_scatter(grad_up, 'fsdp', scatter_dimension=0, tiled=True)  117 us
    reduce_scatter x1, waiting for transfers between devices, per_device(): lax.psum_scatter(grad_down, 'fsdp', scatter_dimension=0, tiled=True)  100 us
    psum x1, waiting for transfers between devices, per_device(): lax.psum(shard_qkv.astype(jnp.bfloat16), 'dp').astype(jnp.float32)  100 us
    all_gather x1, waiting for transfers between devices, per_device(): lax.all_gather(mlp_out, 'fsdp', axis=0, tiled=True)  44 us
    all_gather x1, waiting for transfers between devices, per_device(): lax.all_gather(mlp_in, 'fsdp', axis=0, tiled=True)  38.3 us
    psum x1, blocking collectives, per_device(): grad_router = lax.psum(router_local, ('fsdp', 'dp'))  37.7 us
    dot_general x1, matrix products, per_device(): jnp.einsum('kf,kd->fd', active, grad_expanded, preferred_element_type=jnp...  19 us
  transfers between devices with their start and end apart: 9, of which 6 were waited for; matrix products, arithmetic and copies ran while one was open for 26% of the time, Pallas kernels for 0%

commit v1 on v0

--- a/solution.py
+++ b/solution.py
@@ -7,6 +7,23 @@
 HEAD = 64
 EPS = 1e-06
 MASKED = -1e30
+
+
+def laid_out(pieces, dim):
+    shape = list(pieces.shape[1:])
+    shape[dim] *= pieces.shape[0]
+    return jnp.moveaxis(pieces, 0, dim).reshape(shape)
+
+
+def collect(array, axis, dim):
+    length = lax.axis_size(axis)
+    upward = [(i, (i + 1) % length) for i in range(length)]
+    blocks = [array]
+    while len(blocks) < length:
+        blocks.append(lax.ppermute(blocks[-1], axis, upward))
+    index = lax.axis_index(axis)
+    blocks = jnp.stack(blocks)[(index - jnp.arange(length)) % length]
+    return laid_out(blocks, dim)
 
 
 def rms_scale(values, gain_vec):
@@ -53,10 +70,7 @@
         lax.all_gather(norm_attn, "fsdp", axis=0, tiled=True),
         lax.all_gather(norm_mlp, "fsdp", axis=0, tiled=True),
     )
-    w_in, w_down = (
-        lax.all_gather(mlp_in, "fsdp", axis=0, tiled=True),
-        lax.all_gather(mlp_out, "fsdp", axis=0, tiled=True),
-    )
+    w_in, w_down = (collect(mlp_in, "fsdp", 0), lax.all_gather(mlp_out, "fsdp", axis=0, tiled=True))
     gain_one = gain_attn.astype(jnp.float32)
     gain_two = gain_mlp.astype(jnp.float32)
     positions = lax.broadcasted_iota(jnp.int32, (row_count, tokens.shape[0]), 1)

time: 783 us -> 839 us (1.072)
  waiting for transfers between devices: 411 us -> 443 us
  local copies, waits for them, and re-layouts: 14.3 us -> 32.9 us
  blocking collectives: 84.2 us -> 93.3 us
    ppermute x0 -> x7, waiting for transfers between devices: none -> 121 us  [collect(): blocks.append(lax.ppermute(blocks[-1], axis, upward))]
    all_gather x1, waiting for transfers between devices: 44 us -> 0.01 us  [per_device(): lax.all_gather(mlp_out, 'fsdp', axis=0, tiled=True)]
    all_gather x1, waiting for transfers between devices: 38.3 us -> 0.01 us  [per_device(): lax.all_gather(mlp_in, 'fsdp', axis=0, tiled=True)]
    all_gather x1, blocking collectives: 10.4 us -> 21.2 us  [per_device(): lax.all_gather(norm_attn, 'fsdp', axis=0, tiled=True)]
    unnamed x48 -> x67, local copies, waits for them, and re-layouts: 4.18 us -> 13.5 us
    all_gather x1, waiting for transfers between devices: 8.67 us -> 0.01 us  [per_device(): lax.all_gather(attn_in, 'fsdp', axis=0, tiled=True)]
  transfers between devices with their start and end apart: 9 -> 16, of which waited for: 6 -> 9; matrix products, arithmetic and copies ran while one was open for 26% -> 28% of each run, Pallas kernels for 0% -> 0%
where the time goes in v1:
time: 839 us; the launch traced here: 832 us
  waiting for transfers between devices  443 us (53%)
  matrix products  200 us (24%)
  blocking collectives  93.3 us (11%)
  other arithmetic  43.7 us (5%)
  local copies, waits for them, and re-layouts  32.9 us (4%)
  between operations  15.1 us (2%)
    ppermute x7, waiting for transfers between devices, collect(): blocks.append(lax.ppermute(blocks[-1], axis, upward))  121 us
    reduce_scatter x1, waiting for transfers between devices, per_device(): lax.psum_scatter(grad_up, 'fsdp', scatter_dimension=0, tiled=True)  117 us
    reduce_scatter x1, waiting for transfers between devices, per_device(): lax.psum_scatter(grad_down, 'fsdp', scatter_dimension=0, tiled=True)  102 us
    psum x1, waiting for transfers between devices, per_device(): lax.psum(shard_qkv.astype(jnp.bfloat16), 'dp').astype(jnp.float32)  100 us
    psum x1, blocking collectives, per_device(): grad_router = lax.psum(router_local, ('fsdp', 'dp'))  37.5 us
    all_gather x1, blocking collectives, per_device(): lax.all_gather(norm_attn, 'fsdp', axis=0, tiled=True)  21.2 us
    dot_general x1, matrix products, per_device(): jnp.einsum('kf,kd->fd', active, grad_expanded, preferred_element_type=jnp...  19.3 us
  transfers between devices with their start and end apart: 16, of which 9 were waited for; matrix products, arithmetic and copies ran while one was open for 28% of the time, Pallas kernels for 0%

profile of v1, /device:TPU:0, one launch (start us, length us, event | category | flops | bytes accessed | tf_op | source)
XLA Modules:
  0.0 832.1 jit_solution(5171738749583169594)
XLA Ops:
  10.1 18.8 %collective-permute-done = bf16[128,4096]{1,0:T(8,128)(2,1)S(1)} collective-permute-done((bf16[128,4096]{1,0:T(8,128)(2,1)}, bf16[128,4096]{1,0:T(8,128)(2,1)S(1)}, u32[]{:S(2)}, u32[]{:S(2)}) %collective-permute-start) | collective-permute-done | bytes 1048608 | tf_op jit(solution)/shard_map/ppermute | solution.py:23
  39.0 21.2 %all-gather = bf16[8,1,128]{2,1,0:T(2,128)(2,1)S(1)} all-gather(bf16[1,1,128]{2,1,0:T(2,128)(2,1)S(1)} %bitcast.104), channel_id=1, replica_groups=mesh['fsdp'=8,'dp'=4] {'fsdp'}, dimensions={0}, use_global_device_ids=true | all-gather | bytes 2304 | tf_op jit(solution)/shard_map/all_gather | solution.py:70
  60.2 9.6 %all-gather.1 = bf16[8,1,128]{2,1,0:T(2,128)(2,1)S(1)} all-gather(bf16[1,1,128]{2,1,0:T(2,128)(2,1)S(1)} %bitcast.105), channel_id=1, replica_groups=mesh['fsdp'=8,'dp'=4] {'fsdp'}, dimensions={0}, use_global_device_ids=true | all-gather | bytes 2304 | tf_op jit(solution)/shard_map/all_gather | solution.py:71
  71.2 9.2 %fusion.12 = f32[512,1024]{1,0:T(8,128)} fusion(bf16[4096,1024]{1,0:T(8,128)(2,1)} %param.12, s32[512]{0:T(512)S(1)} %copy-done.11), kind=kOutput, calls=%fused_computation.25 | convolution fusion | flops 4297064448 | bytes 10487808 | tf_op jit(solution)/shard_map/dot_general | solution.py:120
  80.4 8.6 %collective-permute-done.2 = bf16[128,4096]{1,0:T(8,128)(2,1)S(1)} collective-permute-done((bf16[128,4096]{1,0:T(8,128)(2,1)}, bf16[128,4096]{1,0:T(8,128)(2,1)S(1)}, u32[]{:S(2)}, u32[]{:S(2)}) %collective-permute-start.2) | collective-permute-done | bytes 1048608 | tf_op jit(solution)/shard_map/ppermute | solution.py:23
  90.1 19.4 %collective-permute-done.3 = bf16[128,4096]{1,0:T(8,128)(2,1)S(1)} collective-permute-done((bf16[128,4096]{1,0:T(8,128)(2,1)S(1)}, bf16[128,4096]{1,0:T(8,128)(2,1)S(1)}, u32[]{:S(2)}, u32[]{:S(2)}) %collective-permute-start.3) | collective-permute-done | bytes 1048608 | tf_op jit(solution)/shard_map/ppermute | solution.py:23
  112.9 23.0 %collective-permute-done.4 = bf16[128,4096]{1,0:T(8,128)(2,1)S(1)} collective-permute-done((bf16[128,4096]{1,0:T(8,128)(2,1)S(1)}, bf16[128,4096]{1,0:T(8,128)(2,1)S(1)}, u32[]{:S(2)}, u32[]{:S(2)}) %collective-permute-start.4) | collective-permute-done | bytes 1048608 | tf_op jit(solution)/shard_map/ppermute | solution.py:23
  138.0 34.5 %collective-permute-done.5 = bf16[128,4096]{1,0:T(8,128)(2,1)S(1)} collective-permute-done((bf16[128,4096]{1,0:T(8,128)(2,1)S(1)}, bf16[128,4096]{1,0:T(8,128)(2,1)S(1)}, u32[]{:S(2)}, u32[]{:S(2)}) %collective-permute-start.5) | collective-permute-done | bytes 1048608 | tf_op jit(solution)/shard_map/ppermute | solution.py:23
  175.0 16.9 %collective-permute-done.6 = bf16[128,4096]{1,0:T(8,128)(2,1)S(1)} collective-permute-done((bf16[128,4096]{1,0:T(8,128)(2,1)S(1)}, bf16[128,4096]{1,0:T(8,128)(2,1)S(1)}, u32[]{:S(2)}, u32[]{:S(2)}) %collective-permute-start.6) | collective-permute-done | bytes 1048608 | tf_op jit(solution)/shard_map/ppermute | solution.py:23
  192.9 8.2 gather_fusion
  215.5 8.5 %fusion.1 = (f32[16,512]{1,0:T(8,128)S(1)}, f32[16,512,512]{1,2,0:T(8,128)}) fusion(pred[512,512]{0,1:T(8,128)(4,1)S(1)} %compare_and_fusion, bf16[512,16,64]{0,2,1:T(8,128)(2,1)} %bitcast.76, bf16[512,16,64]{0,2,1:T(8,128)(2,1)S(1)} %bitcast.74), kind=kOutput, calls=%fused_computation.12 | convolution fusion | flops 549445632 | bytes 19169280 | tf_op jit(solution)/shard_map/qhd,khd->hqk/dot_general | solution.py:45
  224.0 9.2 %fusion = f32[16,512]{1,0:T(8,128)S(1)} fusion(f32[16,512,512]{1,2,0:T(8,128)} %get-tuple-element.31, f32[16,512]{1,0:T(8,128)S(1)} %get-tuple-element.30, pred[512,512]{0,1:T(8,128)(4,1)S(1)} %compare_and_fusion), kind=kLoop, calls=%fused_computation.9 | loop fusion | flops 16769024 | bytes 17104896 | tf_op jit(solution)/shard_map/reduce_sum | solution.py:91
  233.3 9.2 %fusion.23 = bf16[16,64,512]{2,1,0:T(8,128)(2,1)} fusion(bf16[512,16,64]{0,2,1:T(8,128)(2,1)} %bitcast.85, f32[16,512,512]{1,2,0:T(8,128)} %get-tuple-element.31, f32[16,512]{1,0:T(8,128)S(1)} %fusion, f32[16,512]{1,0:T(8,128)S(1)} %get-tuple-element.30, pred[512,512]{0,1:T(8,128)(4,1)S(1)} %compare_and_fusion), kind=kOutput, calls=%fused_computation.55 | convolution fusion | flops 558366720 | bytes 19202048 | tf_op jit(solution)/shard_map/hqk,khd->qhd/dot_general | solution.py:94
  248.4 10.5 %fusion.52 = f32[512,4096]{1,0:T(8,128)} fusion(bf16[1024,4096]{1,0:T(8,128)(2,1)} %bitcast.78, f32[512,1024]{1,0:T(8,128)S(1)} %get-tuple-element.22, f32[1024]{0:T(1024)S(1)} %bitcast.94, f32[512]{0:T(512)S(1)} %fusion.39), kind=kOutput, calls=%fused_computation.104 | convolution fusion | flops 4296540160 | bytes 18880512 | tf_op jit(solution)/shard_map/dot_general | solution.py:102
  258.8 14.4 %fusion.8 = bf16[512,4096]{1,0:T(8,128)(2,1)} fusion(f32[512,4096]{1,0:T(8,128)} %fusion.52, bf16[4096,1024]{1,0:T(8,128)(2,1)} %all-gather.11.cloned.1.call-done, f32[512,1024]{1,0:T(8,128)} %fusion.12, f32[512]{0:T(512)S(1)} %bitcast.99), kind=kOutput, calls=%fused_computation.19 | convolution fusion | flops 4337958912 | bytes 23070720 | tf_op jit(solution)/shard_map/kd,fd->kf/dot_general | solution.py:125
  273.2 10.1 %multiply_reduce_fusion.1 = (f32[1024]{0:T(1024)S(1)}, f32[512]{0:T(512)S(1)}, f32[512,1024]{1,0:T(8,128)S(1)}) fusion(f32[512,1024]{1,0:T(8,128)} %copy-done.1, f32[512]{0:T(512)S(1)} %fusion.39, f32[1024]{0:T(1024)S(1)} %bitcast.95, bf16[512,4096]{1,0:T(8,128)(2,1)} %fusion.8, bf16[1024,4096]{1,0:T(8,128)(2,1)} %all-gather.13.cloned.1.call-done), kind=kOutput, calls=%fused_computation.40 | convolution fusion | flops 4298111488 | bytes 16789504 | tf_op jit(solution)/shard_map/kf,df->kd/dot_general | solution.py:131
  283.4 10.4 %multiply_reduce_fusion.3 = (f32[512]{0:T(512)S(1)}, bf16[512,1024]{1,0:T(8,128)(2,1)S(1)}, f32[512,1024]{1,0:T(8,128)}) fusion(f32[512,1024]{1,0:T(8,128)S(1)} %copy-done.24, f32[512,1024]{1,0:T(8,128)S(1)} %copy-done.2, f32[512]{0:T(512)S(1)} %multiply_multiply_fusion.3, f32[512]{0:T(512)S(1)} %fusion.39, f32[512,1024]{1,0:T(8,128)S(1)} %get-tuple-element.33, ...), kind=kOutput, calls=%fused_computation.42 | convolution fusion | flops 4319608320 | bytes 28323840 | tf_op jit(solution)/shard_map/dot_general | solution.py:105
  304.6 13.4 %multiply_reduce_fusion = (f32[16,512]{1,0:T(8,128)S(1)}, f32[16,512,512]{1,2,0:T(8,128)}) fusion(f32[16,512]{1,0:T(8,128)S(1)} %log_add_fusion, f32[16,512,512]{1,2,0:T(8,128)} %get-tuple-element.31, pred[512,512]{0,1:T(8,128)(4,1)S(1)} %compare_and_fusion, bf16[512,16,64]{0,2,1:T(8,128)(2,1)} %bitcast.87, bf16[512,16,64]{0,2,1:T(8,128)(2,1)} %bitcast.86), kind=kOutput, calls=%fused_computation.3 | convolution fusion | flops 562028544 | bytes 35979264 | tf_op jit(solution)/shard_map/qhd,khd->hqk/dot_general | solution.py:143
  318.0 13.1 %multiply_convert_fusion = bf16[16,512,512]{1,2,0:T(8,128)(2,1)S(1)} fusion(f32[16,512,512]{1,2,0:T(8,128)} %get-tuple-element.36, f32[16,512]{1,0:T(8,128)S(1)} %get-tuple-element.35, f32[16,512]{1,0:T(8,128)S(1)} %log_add_fusion, f32[16,512,512]{1,2,0:T(8,128)} %get-tuple-element.31, pred[512,512]{0,1:T(8,128)(4,1)S(1)} %compare_and_fusion), kind=kLoop, calls=%fused_computation.2 | loop fusion | flops 29360128 | bytes 42270720 | tf_op jit(solution)/shard_map/convert_element_type | solution.py:147
  335.3 8.7 %fusion.24 = bf16[16,64,512]{2,1,0:T(8,128)(2,1)S(1)} fusion(bf16[512,16,64]{0,2,1:T(8,128)(2,1)S(1)} %bitcast.88, f32[16,512]{1,0:T(8,128)S(1)} %log_add_fusion, f32[16,512,512]{1,2,0:T(8,128)} %get-tuple-element.31, pred[512,512]{0,1:T(8,128)(4,1)S(1)} %compare_and_fusion), kind=kOutput, calls=%fused_computation.57 | convolution fusion | flops 558366720 | bytes 19169280 | tf_op jit(solution)/shard_map/hqk,qhd->khd/dot_general | solution.py:157
  345.0 9.9 %fusion.27 = f32[1024,3072]{1,0:T(8,128)} fusion(bf16[512,1024]{0,1:T(8,128)(2,1)S(1)} %bitcast.108, bf16[512,1024]{0,1:T(8,128)(2,1)S(1)} %bitcast.83, bf16[512,1024]{0,1:T(8,128)(2,1)S(1)} %bitcast.79, f32[512,1024]{1,0:T(8,128)S(1)} %get-tuple-element.29, f32[1024]{0:T(1024)S(1)} %bitcast.91, f32[512]{0:T(512)S(1)} %fusion.38), kind=kOutput, calls=%fused_computation.58 | convolution fusion | flops 3232235520 | bytes 17831936 | tf_op jit(solution)/shard_map/kd,ke->de/dot_general | solution.py:168
  355.0 19.3 %fusion.49 = f32[4096,1024]{1,0:T(8,128)} fusion(f32[512,1024]{1,0:T(8,128)} %fusion.12, f32[512]{0:T(512)S(1)} %bitcast.101, f32[512,4096]{1,0:T(8,128)} %fusion.52), kind=kOutput, calls=%fused_computation.101 | convolution fusion | flops 4314890240 | bytes 27265024 | tf_op jit(solution)/shard_map/kf,kd->fd/dot_general | solution.py:124
  374.6 15.0 %fusion.51 = f32[1024,4096]{1,0:T(8,128)} fusion(bf16[512,4096]{1,0:T(8,128)(2,1)} %fusion.8, f32[512,1024]{1,0:T(8,128)} %copy-done.1, f32[1024]{0:T(1024)S(1)} %bitcast.97, f32[512]{0:T(512)S(1)} %fusion.39), kind=kOutput, calls=%fused_computation.103 | convolution fusion | flops 4296540160 | bytes 23074816 | tf_op jit(solution)/shard_map/kd,kf->df/dot_general | solution.py:130
  391.5 8.4 %multiply_reduce_fusion.2 = (f32[1024]{0:T(1024)S(1)}, f32[512]{0:T(512)S(1)}, f32[512,1024]{1,0:T(8,128)}) fusion(f32[512,1024]{1,0:T(8,128)S(1)} %get-tuple-element.29, f32[512]{0:T(512)S(1)} %fusion.38, f32[1024]{0:T(1024)S(1)} %bitcast.92, bf16[1024,3072]{1,0:T(8,128)(2,1)} %all-gather.7.cloned.1.call-done, bf16[512,1024]{0,1:T(8,128)(2,1)} %bitcast.109, ...), kind=kOutput, calls=%fused_computation.41 | convolution fusion | flops 3233806848 | bytes 13643776 | tf_op jit(solution)/shard_map/ke,de->kd/dot_general | solution.py:169
  400.0 13.3 %all-reduce.2 = (bf16[1024]{0:T(1024)(128)(2,1)S(1)}, bf16[1024]{0:T(1024)(128)(2,1)S(1)}) all-reduce(f32[1024]{0:T(1024)S(1)} %get-tuple-element.11, f32[1024]{0:T(1024)S(1)} %get-tuple-element.9), channel_id=6, replica_groups=mesh['fsdp'=8,'dp'=4] {'fsdp'}, use_global_device_ids=true, to_apply=%region_19.20.clone | all-reduce | flops 2048 | bytes 12288
  413.4 11.7 %all-reduce.3 = (bf16[128]{0:T(256)(128)(2,1)S(1)}, bf16[128]{0:T(256)(128)(2,1)S(1)}) all-reduce(bf16[128]{0:T(256)(128)(2,1)S(1)} %dynamic-slice.7, bf16[128]{0:T(256)(128)(2,1)S(1)} %dynamic-slice.6), channel_id=1, replica_groups=mesh['fsdp'=8,'dp'=4] {'dp'}, use_global_device_ids=true, to_apply=%region_20.21 | all-reduce | flops 256 | bytes 1024 | tf_op jit(solution)/shard_map/psum | solution.py:194
  427.2 37.5 %psum.55 = f32[1024]{0:T(1024)} all-reduce(f32[1024]{0:T(1024)S(1)} %bitcast.89), channel_id=1, replica_groups=mesh['fsdp'=8,'dp'=4] {'fsdp','dp'}, use_global_device_ids=true, to_apply=%region_24.25 | all-reduce | flops 1024 | bytes 8192 | tf_op jit(solution)/shard_map/psum | solution.py:197
  469.4 102.1 %reduce-scatter.11.cloned.1.call-done = f32[512,1024]{1,0:T(8,128)} async-done(((f32[4096,1024]{1,0:T(8,128)}), f32[512,1024]{1,0:T(8,128)}) %reduce-scatter.11.cloned.1.call-update) | async-done | bytes 2097168 | tf_op jit(solution)/shard_map/reduce_scatter | solution.py:181
  574.3 117.0 %reduce-scatter.9.cloned.1.call-done = f32[128,4096]{1,0:T(8,128)} async-done(((f32[1024,4096]{1,0:T(8,128)}), f32[128,4096]{1,0:T(8,128)}) %reduce-scatter.9.cloned.1.call-update) | async-done | bytes 2097168 | tf_op jit(solution)/shard_map/reduce_scatter | solution.py:180
  694.0 10.0 %add_convert_fusion.1 = bf16[4096,1024]{1,0:T(8,128)(2,1)} fusion(bf16[4096,1024]{1,0:T(8,128)(2,1)} %param.11, s32[512]{0:T(512)S(1)} %copy-done.12, f32[512,1024]{1,0:T(8,128)} %get-tuple-element.34, f32[512]{0:T(512)S(1)} %bitcast.102), kind=kOutput, calls=%fused_computation.5 | convolution fusion | flops 4310695936 | bytes 18878464 | tf_op jit(solution)/shard_map/kt,kd->td/dot_general | solution.py:110
  704.1 11.4 %add_convert_fusion = bf16[4096,1024]{1,0:T(8,128)(2,1)} fusion(bf16[4096,1024]{1,0:T(8,128)(2,1)} %param.12, s32[512]{0:T(512)S(1)} %copy-done.12, f32[512,1024]{1,0:T(8,128)S(1)} %get-tuple-element.29, f32[512,1024]{1,0:T(8,128)S(1)} %copy-done.25, f32[1024]{0:T(1024)S(1)} %convert_element_type.135, f32[512]{0:T(512)S(1)} %get-tuple-element.26, ...), kind=kOutput, calls=%fused_computation.1 | convolution fusion | flops 4316987392 | bytes 25190400 | tf_op jit(solution)/shard_map/kt,kd->td/dot_general | solution.py:176
  715.5 100.1 %all-reduce.7.cloned.1.call-done = (bf16[128,3072]{1,0:T(8,128)(2,1)}, bf16[128,1024]{1,0:T(8,128)(2,1)}, bf16[128,4096]{1,0:T(8,128)(2,1)}, bf16[512,1024]{1,0:T(8,128)(2,1)}) async-done(((bf16[128,3072]{1,0:T(8,128)(2,1)}, bf16[128,1024]{1,0:T(8,128)(2,1)}, bf16[128,4096]{1,0:T(8,128)(2,1)}, bf16[512,1024]{1,0:T(8,128)(2,1)}), (bf16[128,3072]{1,0:T(8,128)(2,1)}, bf16[128,1024]{1,0:T(8,128)(2,1)}, ...) | async-done | bytes 3145744 | tf_op jit(solution)/shard_map/psum | solution.py:190
  (137 shorter events, 84.4 us)
Async XLA Ops:
  7.2 193.9 %all-gather.7.cloned.1.call-start = ((), (), s32[]{:S(2)}) async-start(), calls=%async_computation.4 | async-start | bytes 7077888 | tf_op jit(solution)/shard_map/all_gather | solution.py:68
  7.9 234.6 %all-gather.9.cloned.1.call-start = ((), (), s32[]{:S(2)}) async-start(), calls=%async_computation.5 | async-start | bytes 2359296 | tf_op jit(solution)/shard_map/all_gather | solution.py:69
  8.7 250.2 %all-gather.11.cloned.1.call-start = ((), (), s32[]{:S(2)}) async-start(), calls=%async_computation.6 | async-start | bytes 9437184 | tf_op jit(solution)/shard_map/all_gather | solution.py:73
  9.4 263.8 %all-gather.13.cloned.1.call-start = ((), (), s32[]{:S(2)}) async-start(), calls=%async_computation.7 | async-start | bytes 9437184 | tf_op jit(solution)/shard_map/all_gather | solution.py:117
  9.4 19.5 %collective-permute-start = (bf16[128,4096]{1,0:T(8,128)(2,1)}, bf16[128,4096]{1,0:T(8,128)(2,1)S(1)}, u32[]{:S(2)}, u32[]{:S(2)}) collective-permute-start(bf16[128,4096]{1,0:T(8,128)(2,1)} %param.17), channel_id=1, source_target_pairs={{0,4},{4,8},{8,12},{12,16},{16,20},{20,24},{24,28},{28,0},{1,5},{5... | collective-permute-start | bytes 3145736 | tf_op jit(solution)/shard_map/ppermute | solution.py:23
  10.0 29.0 %copy-start.17 = (bf16[128]{0:T(256)(128)(2,1)S(1)}, bf16[128]{0:T(256)(128)(2,1)}, u32[]{:S(2)}) copy-start(bf16[128]{0:T(256)(128)(2,1)} %param.19) | copy-start | bytes 772
  10.0 50.2 %copy-start.18 = (bf16[128]{0:T(256)(128)(2,1)S(1)}, bf16[128]{0:T(256)(128)(2,1)}, u32[]{:S(2)}) copy-start(bf16[128]{0:T(256)(128)(2,1)} %param.20) | copy-start | bytes 772
  10.0 59.8 %copy-start.13 = (bf16[1024]{0:T(1024)(128)(2,1)S(1)}, bf16[1024]{0:T(1024)(128)(2,1)}, u32[]{:S(2)}) copy-start(bf16[1024]{0:T(1024)(128)(2,1)} %param.21) | copy-start | bytes 6148
  10.0 59.8 %copy-start.20 = (s32[8]{0:T(128)S(1)}, s32[8]{0:T(128)}, u32[]{:S(2)}) copy-start(s32[8]{0:T(128)} %param.13) | copy-start | bytes 100
  10.1 60.0 %copy-start.11 = (s32[512]{0:T(512)S(1)}, s32[512]{0:T(512)}, u32[]{:S(2)}) copy-start(s32[512]{0:T(512)} %param.14) | copy-start | bytes 6148
  10.1 454.7 %reduce-scatter.7.cloned.1.call-start = ((), (), s32[]{:S(2)}) async-start(), calls=%async_computation.9 | async-start | bytes 4718592 | tf_op jit(solution)/shard_map/reduce_scatter | solution.py:186
  28.9 41.9 %collective-permute-start.1 = (bf16[128,4096]{1,0:T(8,128)(2,1)S(1)}, bf16[128,4096]{1,0:T(8,128)(2,1)}, u32[]{:S(2)}, u32[]{:S(2)}) collective-permute-start(bf16[128,4096]{1,0:T(8,128)(2,1)S(1)} %collective-permute-done), channel_id=1, source_target_pairs={{0,4},{4,8},{8,12},{12,16},{16,20},{20,24},{24,28},{28,0},{1,5},{5... | collective-permute-start | bytes 3145736 | tf_op jit(solution)/shard_map/ppermute | solution.py:23
  39.0 31.1 %copy-start.15 = (f32[512]{0:T(512)}, f32[512]{0:T(512)S(1)}, u32[]{:S(2)}) copy-start(f32[512]{0:T(512)S(1)} %get-tuple-element.28) | copy-start | bytes 6148
  70.8 18.2 %copy-start.5 = (bf16[128,4096]{1,0:T(8,128)(2,1)S(1)}, bf16[128,4096]{1,0:T(8,128)(2,1)}, u32[]{:S(2)}) copy-start(bf16[128,4096]{1,0:T(8,128)(2,1)} %param.17) | copy-start | bytes 3145732
  70.8 18.2 %collective-permute-start.2 = (bf16[128,4096]{1,0:T(8,128)(2,1)}, bf16[128,4096]{1,0:T(8,128)(2,1)S(1)}, u32[]{:S(2)}, u32[]{:S(2)}) collective-permute-start(bf16[128,4096]{1,0:T(8,128)(2,1)} %collective-permute-done.1), channel_id=1, source_target_pairs={{0,4},{4,8},{8,12},{12,16},{16,20},{20,24},{24,28},{28,0},{1,5},{5... | collective-permute-start | bytes 3145736 | tf_op jit(solution)/shard_map/ppermute | solution.py:23
  89.0 20.5 %collective-permute-start.3 = (bf16[128,4096]{1,0:T(8,128)(2,1)S(1)}, bf16[128,4096]{1,0:T(8,128)(2,1)S(1)}, u32[]{:S(2)}, u32[]{:S(2)}) collective-permute-start(bf16[128,4096]{1,0:T(8,128)(2,1)S(1)} %collective-permute-done.2), channel_id=1, source_target_pairs={{0,4},{4,8},{8,12},{12,16},{16,20},{20,24},{24,28},{28,0},{1,5},{5... | collective-permute-start | bytes 3145736 | tf_op jit(solution)/shard_map/ppermute | solution.py:23
  109.5 26.4 %collective-permute-start.4 = (bf16[128,4096]{1,0:T(8,128)(2,1)S(1)}, bf16[128,4096]{1,0:T(8,128)(2,1)S(1)}, u32[]{:S(2)}, u32[]{:S(2)}) collective-permute-start(bf16[128,4096]{1,0:T(8,128)(2,1)S(1)} %collective-permute-done.3), channel_id=1, source_target_pairs={{0,4},{4,8},{8,12},{12,16},{16,20},{20,24},{24,28},{28,0},{1,5},{5... | collective-permute-start | bytes 3145736 | tf_op jit(solution)/shard_map/ppermute | solution.py:23
  135.8 36.6 %collective-permute-start.5 = (bf16[128,4096]{1,0:T(8,128)(2,1)S(1)}, bf16[128,4096]{1,0:T(8,128)(2,1)S(1)}, u32[]{:S(2)}, u32[]{:S(2)}) collective-permute-start(bf16[128,4096]{1,0:T(8,128)(2,1)S(1)} %collective-permute-done.4), channel_id=1, source_target_pairs={{0,4},{4,8},{8,12},{12,16},{16,20},{20,24},{24,28},{28,0},{1,5},{5... | collective-permute-start | bytes 3145736 | tf_op jit(solution)/shard_map/ppermute | solution.py:23
  172.4 19.4 %collective-permute-start.6 = (bf16[128,4096]{1,0:T(8,128)(2,1)S(1)}, bf16[128,4096]{1,0:T(8,128)(2,1)S(1)}, u32[]{:S(2)}, u32[]{:S(2)}) collective-permute-start(bf16[128,4096]{1,0:T(8,128)(2,1)S(1)} %collective-permute-done.5), channel_id=1, source_target_pairs={{0,4},{4,8},{8,12},{12,16},{16,20},{20,24},{24,28},{28,0},{1,5},{5... | collective-permute-start | bytes 3145736 | tf_op jit(solution)/shard_map/ppermute | solution.py:23
  273.2 10.2 %copy-start.4 = (f32[512,1024]{1,0:T(8,128)S(1)}, f32[512,1024]{1,0:T(8,128)}, u32[]{:S(2)}) copy-start(f32[512,1024]{1,0:T(8,128)} %get-tuple-element.32) | copy-start | bytes 6291460
  273.2 10.2 %copy-start.19 = (bf16[4096,1024]{1,0:T(8,128)(2,1)S(1)}, bf16[4096,1024]{1,0:T(8,128)(2,1)}, u32[]{:S(2)}) copy-start(bf16[4096,1024]{1,0:T(8,128)(2,1)} %all-gather.11.cloned.1.call-done) | copy-start | bytes 25165828
  273.2 10.2 %copy-start.24 = (f32[512,1024]{1,0:T(8,128)S(1)}, f32[512,1024]{1,0:T(8,128)}, u32[]{:S(2)}) copy-start(f32[512,1024]{1,0:T(8,128)} %fusion.12) | copy-start | bytes 6291460
  283.4 10.4 %copy-start.26 = (f32[512,1024]{1,0:T(8,128)}, f32[512,1024]{1,0:T(8,128)S(1)}, u32[]{:S(2)}) copy-start(f32[512,1024]{1,0:T(8,128)S(1)} %get-tuple-element.33) | copy-start | bytes 6291460
  283.4 11.4 %copy-start.8 = (bf16[16,64,512]{2,1,0:T(8,128)(2,1)S(1)}, bf16[16,64,512]{2,1,0:T(8,128)(2,1)}, u32[]{:S(2)}) copy-start(bf16[16,64,512]{2,1,0:T(8,128)(2,1)} %fusion.23) | copy-start | bytes 3145732
  304.6 162.1 %reduce-scatter.5.cloned.1.call-start = ((), (), s32[]{:S(2)}) async-start(), calls=%async_computation.8 | async-start | bytes 14155776 | tf_op jit(solution)/shard_map/reduce_scatter | solution.py:185
  318.0 13.1 %copy-start = (bf16[512,1024]{0,1:T(8,128)(2,1)S(1)}, bf16[512,1024]{0,1:T(8,128)(2,1)}, u32[]{:S(2)}) copy-start(bf16[512,1024]{0,1:T(8,128)(2,1)} %copy.49) | copy-start | bytes 3145732
  333.7 10.3 %copy-start.9 = (bf16[16,64,512]{2,1,0:T(8,128)(2,1)}, bf16[16,64,512]{2,1,0:T(8,128)(2,1)S(1)}, u32[]{:S(2)}) copy-start(bf16[16,64,512]{2,1,0:T(8,128)(2,1)S(1)} %multiply_convert_fusion.2) | copy-start | bytes 3145732
  354.9 216.6 %reduce-scatter.11.cloned.1.call-start = ((), (), s32[]{:S(2)}) async-start(), calls=%async_computation.11 | async-start | bytes 18874368 | tf_op jit(solution)/shard_map/reduce_scatter | solution.py:181
  374.3 317.0 %reduce-scatter.9.cloned.1.call-start = ((), (), s32[]{:S(2)}) async-start(), calls=%async_computation.10 | async-start | bytes 18874368 | tf_op jit(solution)/shard_map/reduce_scatter | solution.py:180
  389.6 426.0 %all-reduce.7.cloned.1.call-start = ((), (), s32[]{:S(2)}) async-start(), calls=%async_computation.12 | async-start | bytes 6291456 | tf_op jit(solution)/shard_map/psum | solution.py:190
  391.5 73.3 %copy-start.16 = (f32[512]{0:T(512)S(1)}, f32[512]{0:T(512)}, u32[]{:S(2)}) copy-start(f32[512]{0:T(512)} %copy-done.15) | copy-start | bytes 6148
  400.0 294.0 %copy-start.12 = (s32[512]{0:T(512)S(1)}, s32[512]{0:T(512)}, u32[]{:S(2)}) copy-start(s32[512]{0:T(512)} %param.14) | copy-start | bytes 6148
  (12 other events, 57.3 us)
Sparse Core Ops, SparseCore 0:
  9.9 56.8 all-gather.6
  68.6 33.1 all-gather.8
  103.7 69.3 all-gather.10
  174.8 55.5 all-gather.12
  304.7 50.3 reduce-scatter.6
  358.5 93.2 reduce-scatter.4
  455.4 116.1 reduce-scatter.10
  575.1 116.1 reduce-scatter.8
  694.5 121.0 all-reduce.6
